TPU v7x, 128 devices: a whole 4x4x4 slice. The times are simulated.
128 devices in a mesh: sub: 128 (over z, y, x, core).
Axes of the slice: x: 4, y: 4, z: 4, core: 2. Of those that a mesh axis runs over, the one named last changes fastest.
Arguments:
- pool_inputs: bfloat16 [65536, 4096], P('sub'), may hold values from -6 to 6
- pool_targets: bfloat16 [65536, 4096], P('sub'), may hold values from -6 to 6
- row_picks: int32 [8, 32768], P(None, 'sub'), may hold values from 0 to 511
- weight_in: float32 [4096, 32768], P(None, 'sub'), may hold values from -6 to 6
- weight_out: float32 [4096, 32768], P(None, 'sub'), may hold values from -6 to 6
- eval_inputs: bfloat16 [256, 4096], P('sub'), may hold values from -6 to 6
- handover: int32 [4096], replicated, may hold values from 0 to 4095, as said below
Outputs:
- trained_in: float32 [4096, 32768], P(None, 'sub')
- trained_out: float32 [4096, 32768], P(None, 'sub')
- prediction: float32 [256, 4096], P('sub')
Inputs may be any that keep to these rules, and one draw needn't show every extreme that they name: `row_picks`: indices into the subnet's own 512 resident rows. handover[g] is the new position of neuron group g (neurons 8 g to 8 g + 7); every position is taken once, and no two groups of one subnet move to the same subnet.
All inputs are finite; a program needn't handle non-finite values.
Results may differ from a plain program's by a relative error of at most 0.0065.
Values may be sent and summed in bfloat16 or wider, within the bound.
No kernel may reach another device: no remote copies, remote signals or barrier semaphores. Data moves between devices by JAX's collectives and lax.ppermute only.
A program may use at most 192 MiB of HBM per device.

v0:
```python
import math

import jax
import jax.numpy as jnp
from jax import lax
from jax.experimental import pallas as pl
from jax.experimental.pallas import tpu as pltpu
from jax.sharding import PartitionSpec as P

D = 4096
GROUP = 8
STEPS = 4


tanh_coef = 0.7978845608028654
cubic_coef = 0.044715
step_rate = 0.5


def gelu_value(inputs):
    inner_term = tanh_coef * (inputs + cubic_coef * inputs * inputs * inputs)
    return 0.5 * inputs * (1.0 + jnp.tanh(inner_term))


def gelu_parts(inputs):
    tanh_part = jnp.tanh(tanh_coef * (inputs + cubic_coef * inputs * inputs * inputs))
    values = 0.5 * inputs * (1.0 + tanh_part)
    slopes = 0.5 * (1.0 + tanh_part) + 0.5 * inputs * (1.0 - tanh_part * tanh_part) * tanh_coef * (
        1.0 + 3.0 * cubic_coef * inputs * inputs
    )
    return (values, slopes)


NT = (((1,), (1,)), ((), ()))


def train_steps(scale_in, scale_out, picks_ref, pin_ref, ptg_ref, wi_ref, wo_ref, rows_ref):
    batch = picks_ref.shape[0]
    pool = pin_ref.shape[0]
    turns = picks_ref.shape[1]

    def one_turn(turn, carry):
        lanes = lax.broadcasted_iota(jnp.int32, (batch, turns), 1)
        picked = jnp.sum(jnp.where(lanes == turn, picks_ref[...], 0), axis=1, keepdims=True)
        onehot = (picked == lax.broadcasted_iota(jnp.int32, (batch, pool), 1)).astype(jnp.bfloat16)
        rows = jnp.dot(onehot, pin_ref[...], preferred_element_type=jnp.float32).astype(jnp.bfloat16)
        rows_ref[...] = rows
        in_half = wi_ref[...].astype(jnp.bfloat16)
        before = lax.dot_general(rows, in_half, NT, preferred_element_type=jnp.float32) * scale_in
        values, slopes = gelu_parts(before)
        activity = values.astype(jnp.bfloat16)
        activity_t = values.T.astype(jnp.bfloat16)
        goals = jnp.dot(onehot, ptg_ref[...], preferred_element_type=jnp.float32)
        out_half = wo_ref[...].astype(jnp.bfloat16)
        branch = jnp.dot(activity, out_half, preferred_element_type=jnp.float32) * scale_out
        errors = (branch - goals).astype(jnp.bfloat16)
        back = lax.dot_general(errors, out_half, NT, preferred_element_type=jnp.float32)
        grad_out = jnp.dot(activity_t, errors, preferred_element_type=jnp.float32) * scale_out
        wo_ref[...] = wo_ref[...] - step_rate * grad_out
        backward = back * scale_out * slopes
        backward_t = backward.astype(jnp.bfloat16).astype(jnp.float32).T.astype(jnp.bfloat16)
        grad_in = jnp.dot(backward_t, rows_ref[...], preferred_element_type=jnp.float32) * scale_in
        wi_ref[...] = wi_ref[...] - step_rate * grad_in
        return carry

    lax.fori_loop(0, turns, one_turn, 0)


def first_body(scale_in, scale_out, picks_ref, pin_ref, ptg_ref, wi0_ref, wo0_ref,
               inh_ref, outh_ref, wi_ref, wo_ref, rows_ref):
    wi_ref[...] = wi0_ref[...].T
    wo_ref[...] = wo0_ref[...].T
    train_steps(scale_in, scale_out, picks_ref, pin_ref, ptg_ref, wi_ref, wo_ref, rows_ref)
    inh_ref[...] = wi_ref[...].astype(jnp.bfloat16)
    outh_ref[...] = wo_ref[...].astype(jnp.bfloat16)


def second_body(scale_in, scale_out, src_ref, picks_ref, pin_ref, ptg_ref, land_ref,
                ti_ref, to_ref, wi_ref, wo_ref, rows_ref, stage_ref, sems):
    groups = stage_ref.shape[0]

    def fetch(g, carry):
        pltpu.make_async_copy(land_ref.at[src_ref[g]], stage_ref.at[g], sems.at[g]).start()
        return carry

    lax.fori_loop(0, groups, fetch, 0)

    def unpack(g, carry):
        pltpu.make_async_copy(land_ref.at[src_ref[g]], stage_ref.at[g], sems.at[g]).wait()
        block = stage_ref[g].astype(jnp.float32)
        part = pl.ds(pl.multiple_of(g * GROUP, GROUP), GROUP)
        wi_ref[part, :] = block[:GROUP]
        wo_ref[part, :] = block[GROUP:]
        return carry

    lax.fori_loop(0, groups, unpack, 0)
    train_steps(scale_in, scale_out, picks_ref, pin_ref, ptg_ref, wi_ref, wo_ref, rows_ref)
    ti_ref[...] = wi_ref[...].T
    to_ref[...] = wo_ref[...].T


def round_cost(hidden, width, batch, turns, pool):
    flops = turns * 2 * (2 * batch * pool * width + 5 * batch * hidden * width)
    return pl.CostEstimate(
        flops=flops,
        transcendentals=turns * batch * hidden,
        bytes_accessed=4 * hidden * width * 4 + 2 * pool * width * 2,
    )


VMEM_LIMIT = 63 * 1024 * 1024


def first_round(picks_t, pool_inputs, pool_targets, weight_in, weight_out, scale_in, scale_out):
    width, hidden = weight_in.shape
    batch, turns = picks_t.shape
    pool = pool_inputs.shape[0]
    vmem = pl.BlockSpec(memory_space=pltpu.VMEM)
    return pl.pallas_call(
        lambda *refs: first_body(scale_in, scale_out, *refs),
        out_shape=(
            jax.ShapeDtypeStruct((hidden, width), jnp.bfloat16),
            jax.ShapeDtypeStruct((hidden, width), jnp.bfloat16),
        ),
        in_specs=[vmem] * 5,
        out_specs=(vmem, vmem),
        scratch_shapes=[
            pltpu.VMEM((hidden, width), jnp.float32),
            pltpu.VMEM((hidden, width), jnp.float32),
            pltpu.VMEM((batch, width), jnp.bfloat16),
        ],
        compiler_params=pltpu.CompilerParams(vmem_limit_bytes=VMEM_LIMIT),
        cost_estimate=round_cost(hidden, width, batch, turns, pool),
        name="first_round",
    )(picks_t, pool_inputs, pool_targets, weight_in, weight_out)


def second_round(sources, picks_t, pool_inputs, pool_targets, landed, hidden, scale_in, scale_out):
    _, _, width = landed.shape
    batch, turns = picks_t.shape
    pool = pool_inputs.shape[0]
    groups = hidden // GROUP
    vmem = pl.BlockSpec(memory_space=pltpu.VMEM)
    return pl.pallas_call(
        lambda *refs: second_body(scale_in, scale_out, *refs),
        out_shape=(
            jax.ShapeDtypeStruct((width, hidden), jnp.float32),
            jax.ShapeDtypeStruct((width, hidden), jnp.float32),
        ),
        in_specs=[pl.BlockSpec(memory_space=pltpu.SMEM), vmem, vmem, vmem,
                  pl.BlockSpec(memory_space=pl.ANY)],
        out_specs=(vmem, vmem),
        scratch_shapes=[
            pltpu.VMEM((hidden, width), jnp.float32),
            pltpu.VMEM((hidden, width), jnp.float32),
            pltpu.VMEM((batch, width), jnp.bfloat16),
            pltpu.VMEM((groups, 2 * GROUP, width), jnp.bfloat16),
            pltpu.SemaphoreType.DMA((groups,)),
        ],
        compiler_params=pltpu.CompilerParams(vmem_limit_bytes=VMEM_LIMIT),
        cost_estimate=round_cost(hidden, width, batch, turns, pool),
        name="second_round",
    )(sources, picks_t, pool_inputs, pool_targets, landed)


def per_device(pool_inputs, pool_targets, row_picks, weight_in, weight_out, eval_inputs, handover):
    owners = lax.axis_size("sub")
    my_index = lax.axis_index("sub")
    hidden = weight_in.shape[1]
    group_count = hidden // GROUP
    scale_in = 1.0 / math.sqrt(D)
    scale_out = 1.0 / math.sqrt(hidden * owners)
    picks_t = row_picks.T
    in_half, out_half = first_round(
        picks_t[:, :STEPS], pool_inputs, pool_targets, weight_in, weight_out, scale_in, scale_out
    )
    pieces = owners
    piece = 2 * GROUP * D // pieces
    splits = pieces // (2 * GROUP)
    stacked = jnp.concatenate(
        [in_half.reshape(group_count, GROUP, D), out_half.reshape(group_count, GROUP, D)], axis=1
    )
    spread = (
        stacked.reshape(group_count, 2 * GROUP, splits, piece)
        .transpose(1, 2, 0, 3)
        .reshape(pieces, group_count, piece)
    )
    eval_rows = eval_inputs.shape[0]
    eval_pieces = eval_rows * D // piece
    eval_spread = jnp.broadcast_to(
        eval_inputs.reshape(1, eval_pieces, piece), (pieces, eval_pieces, piece)
    )
    held_all = lax.all_to_all(
        jnp.concatenate([spread, eval_spread], axis=1), "sub", 0, 0, tiled=True
    )
    held = held_all[:, :group_count].reshape(owners * group_count, piece)
    eval_all = held_all[:, group_count:].reshape(owners * eval_rows, D)
    forward = (
        jnp.zeros_like(held)
        .at[handover]
        .set(held, unique_indices=True)
        .reshape(owners, group_count, piece)
    )
    arrived = lax.all_to_all(forward, "sub", 0, 0, tiled=True)
    landed = (
        arrived.reshape(2 * GROUP, splits, group_count, piece)
        .transpose(2, 0, 1, 3)
        .reshape(group_count, 2 * GROUP, D)
    )
    eval_act = gelu_value(
        lax.dot_general(eval_all, in_half, NT, preferred_element_type=jnp.float32) * scale_in
    ).astype(jnp.bfloat16)
    partial = jnp.dot(eval_act, out_half, preferred_element_type=jnp.float32) * scale_out
    rows_each = partial.shape[0] // owners
    parity = my_index % 2
    split = partial.reshape(owners // 2, 2, rows_each, partial.shape[1])
    mine = jnp.where(parity == 0, split[:, 0], split[:, 1])
    other = jnp.where(parity == 0, split[:, 1], split[:, 0])
    mine, other, landed = lax.optimization_barrier((mine, other, landed))
    pairs = [(k, k ^ 1) for k in range(owners)]
    summed = mine + lax.ppermute(other, "sub", perm=pairs)
    same_parity = [list(range(0, owners, 2)), list(range(1, owners, 2))]
    gathered = lax.all_to_all(summed, "sub", 0, 0, tiled=True, axis_index_groups=same_parity)
    prediction = jnp.sum(gathered, axis=0)

    sources = jnp.arange(group_count, dtype=jnp.int32)
    trained_in, trained_out = second_round(
        sources, picks_t[:, STEPS:], pool_inputs, pool_targets, landed, hidden, scale_in, scale_out
    )
    return (trained_in, trained_out, prediction)


def solution(mesh):
    in_specs = (
        P("sub", None),
        P("sub", None),
        P(None, "sub"),
        P(None, "sub"),
        P(None, "sub"),
        P("sub", None),
        P(),
    )
    out_specs = (P(None, "sub"), P(None, "sub"), P("sub", None))
    return jax.shard_map(
        per_device, mesh=mesh, in_specs=in_specs, out_specs=out_specs, check_vma=False
    )
```

profile of v0, /device:TPU:84, one launch (start us, length us, event | category | flops | bytes accessed | tf_op | source)
XLA Modules:
  0.0 278.3 jit_solution(2241176410056170083)
XLA Ops:
  2.2 32.1 %first_round.1 = (bf16[256,4096]{1,0:T(8,128)(2,1)}, bf16[256,4096]{1,0:T(8,128)(2,1)}) custom-call(s32[256,4]{1,0:T(8,128)} %get-tuple-element.17.refs_0_, bf16[512,4096]{1,0:T(8,128)(2,1)} %refs_2_.3, bf16[512,4096]{1,0:T(8,128)(2,1)} %refs_3_.3, f32[4096,256]{1,0:T(8,128)} %refs_3_.2, f32[4096,256]{1,0:T(8,128)} %refs_4_.1), custom_call_target="tpu_custom_call" | custom-call | flops 19327352832 | bytes 25165824 | tf_op jit(solution)/shard_map/first_round/pallas_call | solution.py:119
  34.3 2.9 %copy.16 = bf16[32,8,8,512]{3,0,2,1:T(8,128)(2,1)S(1)} copy(bf16[32,8,8,512]{3,1,2,0:T(8,128)(2,1)} %bitcast.36) | data formatting | bytes 4194304 | tf_op jit(solution)/shard_map/concatenate | solution.py:180
  37.2 2.5 copy.17
  39.7 2.0 pad_maximum_fusion.1
  42.0 3.1 %pad_maximum_fusion = bf16[128,48,512]{2,1,0:T(8,128)(2,1)} fusion(bf16[128,16,512]{2,1,0:T(8,128)(2,1)S(1)} %broadcast_in_dim.14, bf16[128,32,512]{2,1,0:T(8,128)(2,1)S(1)} %bitcast.33), kind=kLoop, calls=%fused_computation.1 | loop fusion | flops 12582912 | bytes 12582912 | tf_op jit(solution)/shard_map/concatenate | solution.py:194
  45.1 10.3 %all-to-all-start = ((bf16[128,48,512]{2,1,0:T(8,128)(2,1)}), bf16[128,48,512]{2,1,0:T(8,128)(2,1)}, u32[]{:S(2)}, u32[]{:S(2)}) async-start(bf16[128,48,512]{2,1,0:T(8,128)(2,1)} %pad_maximum_fusion), calls=%async_computation | async-start | bytes 12582912 | tf_op jit(solution)/shard_map/all_to_all | solution.py:193
  55.4 69.9 %all-to-all-done = bf16[128,48,512]{2,1,0:T(8,128)(2,1)} async-done(((bf16[128,48,512]{2,1,0:T(8,128)(2,1)}), bf16[128,48,512]{2,1,0:T(8,128)(2,1)}, u32[]{:S(2)}, u32[]{:S(2)}) %all-to-all-start) | async-done | bytes 6291488 | tf_op jit(solution)/shard_map/all_to_all | solution.py:193
  125.3 4.8 %slice.31 = bf16[128,32,512]{2,1,0:T(8,128)(2,1)} slice(bf16[128,48,512]{2,1,0:T(8,128)(2,1)} %all-to-all-done), slice={[0:128], [0:32], [0:512]} | slice | bytes 8388608 | tf_op jit(solution)/shard_map/slice | solution.py:196
  130.1 21.3 %scatter_custom_fusion = bf16[4096,512]{1,0:T(8,128)(2,1)} fusion(s32[4096]{0:T(1024)S(1)} %compare_select_fusion, bf16[4096,512]{1,0:T(8,128)(2,1)} %bitcast.38, bf16[]{:T(256)} %constant.36.clone.1), kind=kCustom, calls=%fused_computation.9 | custom fusion | bytes 4194816 | tf_op jit(solution)/shard_map/scatter | solution.py:201
  151.4 11.4 %all-to-all-start.1 = ((bf16[128,32,512]{2,1,0:T(8,128)(2,1)}), bf16[128,32,512]{2,1,0:T(8,128)(2,1)}, u32[]{:S(2)}, u32[]{:S(2)}) async-start(bf16[128,32,512]{2,1,0:T(8,128)(2,1)} %bitcast.34), calls=%async_computation.1 | async-start | bytes 8388608 | tf_op jit(solution)/shard_map/all_to_all | solution.py:204
  162.9 3.2 %slice.28 = bf16[128,16,512]{2,1,0:T(8,128)(2,1)} slice(bf16[128,48,512]{2,1,0:T(8,128)(2,1)} %all-to-all-done), slice={[0:128], [32:48], [0:512]} | slice | bytes 4194304 | tf_op jit(solution)/shard_map/slice | solution.py:197
  166.1 4.2 %reshape.41 = bf16[256,4096]{1,0:T(8,128)(2,1)} reshape(bf16[128,16,512]{2,1,0:T(8,128)(2,1)} %slice.28) | data formatting | bytes 4194304 | tf_op jit(solution)/shard_map/reshape | solution.py:197
  170.3 6.7 %convolution_multiply_fusion = f32[256,4096]{1,0:T(8,128)} fusion(bf16[256,4096]{1,0:T(8,128)(2,1)} %get-tuple-element.11, bf16[256,4096]{1,0:T(8,128)(2,1)} %reshape.41, bf16[256,4096]{1,0:T(8,128)(2,1)S(1)} %copy-done.1), kind=kOutput, calls=%fused_computation.2 | convolution fusion | flops 1075445760 | bytes 10485760 | tf_op jit(solution)/shard_map/dot_general | solution.py:213
  177.0 5.8 %reshape.42 = f32[64,2,2,4096]{3,2,1,0:T(2,128)} reshape(f32[256,4096]{1,0:T(8,128)} %convolution_multiply_fusion) | data formatting | bytes 8388608 | tf_op jit(solution)/shard_map/reshape | solution.py:216
  182.9 5.9 %fusion = f32[64,2,4096]{2,1,0:T(2,128)} fusion(pred[]{:T(512)S(6)} %eq.6, f32[64,2,2,4096]{3,2,1,0:T(2,128)} %reshape.42), kind=kLoop, calls=%fused_computation.6 | loop fusion | flops 524288 | bytes 6291457 | tf_op jit(solution)/shard_map/jit(_where)/select_n | solution.py:218
  188.7 1.5 fusion.1
  190.2 19.1 %all-to-all-done.1 = bf16[128,32,512]{2,1,0:T(8,128)(2,1)} async-done(((bf16[128,32,512]{2,1,0:T(8,128)(2,1)}), bf16[128,32,512]{2,1,0:T(8,128)(2,1)}, u32[]{:S(2)}, u32[]{:S(2)}) %all-to-all-start.1) | async-done | bytes 4194336 | tf_op jit(solution)/shard_map/all_to_all | solution.py:204
  209.4 6.5 %copy.25 = bf16[16,8,32,512]{3,1,0,2:T(8,128)(2,1)} copy(bf16[16,8,32,512]{3,2,1,0:T(8,128)(2,1)} %bitcast.12) | data formatting | bytes 8388608 | tf_op jit(solution)/shard_map/reshape | solution.py:206
  215.9 7.4 %reshape.46.refs_4_ = bf16[32,16,4096]{2,1,0:T(8,128)(2,1)} reshape(bf16[32,16,8,512]{3,2,1,0:T(8,128)(2,1)} %bitcast.35) | data formatting | bytes 8388608 | tf_op jit(solution)/shard_map/reshape | solution.py:208
  223.3 4.4 %collective-permute-done = f32[64,2,4096]{2,1,0:T(2,128)S(1)} collective-permute-done((f32[64,2,4096]{2,1,0:T(2,128)}, f32[64,2,4096]{2,1,0:T(2,128)S(1)}, u32[]{:S(2)}, u32[]{:S(2)}) %collective-permute-start) | collective-permute-done | bytes 2097184 | tf_op jit(solution)/shard_map/ppermute | solution.py:221
  227.7 2.8 %add.28 = f32[64,2,4096]{2,1,0:T(2,128)} add(f32[64,2,4096]{2,1,0:T(2,128)S(1)} %fusion.1, f32[64,2,4096]{2,1,0:T(2,128)S(1)} %collective-permute-done) | non-fusion elementwise | flops 524288 | bytes 6291456 | tf_op jit(solution)/shard_map/add | solution.py:221
  230.5 11.9 %all-to-all-start.2 = ((f32[64,2,4096]{2,1,0:T(2,128)}), f32[64,2,4096]{2,1,0:T(2,128)}, u32[]{:S(2)}, u32[]{:S(2)}) async-start(f32[64,2,4096]{2,1,0:T(2,128)} %add.28), calls=%async_computation.2 | async-start | bytes 4194304 | tf_op jit(solution)/shard_map/all_to_all | solution.py:223
  243.0 32.5 %second_round.1 = (f32[4096,256]{1,0:T(8,128)}, f32[4096,256]{1,0:T(8,128)}) custom-call(s32[32]{0:T(128)} %iota.3.refs_0_, s32[256,4]{1,0:T(8,128)} %get-tuple-element.18.refs_1_, bf16[512,4096]{1,0:T(8,128)(2,1)} %refs_2_.3, bf16[512,4096]{1,0:T(8,128)(2,1)} %refs_3_.3, bf16[32,16,4096]{2,1,0:T(8,128)(2,1)} %reshape.46.refs_4_), custom_call_target="tpu_custom_call" | custom-call | flops 19327352832 | bytes 25165824 | tf_op jit(solution)/shard_map/second_round/pallas_call | solution.py:144
  275.5 2.8 %reduce_sum.9 = f32[2,4096]{1,0:T(2,128)} reduce(f32[64,2,4096]{2,1,0:T(2,128)} %all-to-all-done.2, f32[]{:T(128)} %constant.38.clone.1), dimensions={0}, to_apply=%region_1.2 | reduce | flops 516096 | bytes 2129924 | tf_op jit(solution)/shard_map/reduce_sum | solution.py:224
  (18 shorter events, 2.4 us)
Async XLA Ops:
  34.3 2.9 %copy-start.2 = (bf16[256,4096]{1,0:T(8,128)(2,1)S(1)}, bf16[256,4096]{1,0:T(8,128)(2,1)}, u32[]{:S(2)}) copy-start(bf16[256,4096]{1,0:T(8,128)(2,1)} %get-tuple-element.11) | copy-start | bytes 6291460
  34.3 5.4 %copy-start.3 = (bf16[2,4096]{1,0:T(2,128)(2,1)S(1)}, bf16[2,4096]{1,0:T(2,128)(2,1)}, u32[]{:S(2)}) copy-start(bf16[2,4096]{1,0:T(2,128)(2,1)} %param.12) | copy-start | bytes 49156
  45.1 10.3 %copy-start.4 = (s32[4096]{0:T(1024)S(1)}, s32[4096]{0:T(1024)}, u32[]{:S(2)}) copy-start(s32[4096]{0:T(1024)} %param.13) | copy-start | bytes 49156
  45.1 80.3 %all-to-all-start = ((bf16[128,48,512]{2,1,0:T(8,128)(2,1)}), bf16[128,48,512]{2,1,0:T(8,128)(2,1)}, u32[]{:S(2)}, u32[]{:S(2)}) async-start(bf16[128,48,512]{2,1,0:T(8,128)(2,1)} %pad_maximum_fusion), calls=%async_computation | async-start | bytes 12582912 | tf_op jit(solution)/shard_map/all_to_all | solution.py:193
  151.4 57.9 %all-to-all-start.1 = ((bf16[128,32,512]{2,1,0:T(8,128)(2,1)}), bf16[128,32,512]{2,1,0:T(8,128)(2,1)}, u32[]{:S(2)}, u32[]{:S(2)}) async-start(bf16[128,32,512]{2,1,0:T(8,128)(2,1)} %bitcast.34), calls=%async_computation.1 | async-start | bytes 8388608 | tf_op jit(solution)/shard_map/all_to_all | solution.py:204
  162.9 7.5 %copy-start.1 = (bf16[256,4096]{1,0:T(8,128)(2,1)S(1)}, bf16[256,4096]{1,0:T(8,128)(2,1)}, u32[]{:S(2)}) copy-start(bf16[256,4096]{1,0:T(8,128)(2,1)} %get-tuple-element.10) | copy-start | bytes 6291460
  182.9 5.9 %copy-start = (f32[64,2,2,4096]{3,2,1,0:T(2,128)S(1)}, f32[64,2,2,4096]{3,2,1,0:T(2,128)}, u32[]{:S(2)}) copy-start(f32[64,2,2,4096]{3,2,1,0:T(2,128)} %reshape.42) | copy-start | bytes 12582916
  223.3 4.4 %collective-permute-start = (f32[64,2,4096]{2,1,0:T(2,128)}, f32[64,2,4096]{2,1,0:T(2,128)S(1)}, u32[]{:S(2)}, u32[]{:S(2)}) collective-permute-start(f32[64,2,4096]{2,1,0:T(2,128)} %fusion), channel_id=1, source_target_pairs={{0,1},{1,0},{2,3},{3,2},{4,5},{5,4},{6,7},{7,6},{8,9},{9,8},{10,11... | collective-permute-start | bytes 6291464 | tf_op jit(solution)/shard_map/ppermute | solution.py:221
  230.5 44.9 %all-to-all-start.2 = ((f32[64,2,4096]{2,1,0:T(2,128)}), f32[64,2,4096]{2,1,0:T(2,128)}, u32[]{:S(2)}, u32[]{:S(2)}) async-start(f32[64,2,4096]{2,1,0:T(2,128)} %add.28), calls=%async_computation.2 | async-start | bytes 4194304 | tf_op jit(solution)/shard_map/all_to_all | solution.py:223
where the time goes:
time: 281 us; the launch traced here: 278 us
  waiting for transfers between devices  93.4 us (33%)
  Pallas kernels  64.6 us (23%)
  local copies, waits for them, and re-layouts  61.1 us (22%)
  starting transfers between devices  33.7 us (12%)
  other arithmetic  18.1 us (6%)
  matrix products  6.67 us (2%)
    all_to_all x1, waiting for transfers between devices, per_device(): lax.all_to_all(jnp.concatenate([spread, eval_spread], axis=1), 'sub', 0,...  69.9 us
    pallas_call x1, Pallas kernels, second_round(): pl.pallas_call(lambda *refs: second_body(scale_in, scale_out, *refs), out...  32.5 us
    pallas_call x1, Pallas kernels, first_round(): pl.pallas_call(lambda *refs: first_body(scale_in, scale_out, *refs), out_...  32.1 us
    scatter x1, local copies, waits for them, and re-layouts, per_device(): forward = jnp.zeros_like(held).at[handover].set(held, unique_indices=True...  21.3 us
    all_to_all x1, waiting for transfers between devices, per_device(): arrived = lax.all_to_all(forward, 'sub', 0, 0, tiled=True)  19.1 us
    all_to_all x1, starting transfers between devices, per_device(): lax.all_to_all(summed, 'sub', 0, 0, tiled=True, axis_index_groups=same_pa...  11.9 us
    all_to_all x1, starting transfers between devices, per_device(): arrived = lax.all_to_all(forward, 'sub', 0, 0, tiled=True)  11.4 us
    all_to_all x1, starting transfers between devices, per_device(): lax.all_to_all(jnp.concatenate([spread, eval_spread], axis=1), 'sub', 0,...  10.3 us
  transfers between devices with their start and end apart: 4, of which 3 were waited for; matrix products, arithmetic and copies ran while one was open for 10% of the time, Pallas kernels for 12%

commit v1 on v0

--- a/solution.py
+++ b/solution.py
@@ -195,12 +195,13 @@
     )
     held = held_all[:, :group_count].reshape(owners * group_count, piece)
     eval_all = held_all[:, group_count:].reshape(owners * eval_rows, D)
-    forward = (
-        jnp.zeros_like(held)
+    total_groups = owners * group_count
+    inverse = (
+        jnp.zeros((total_groups,), jnp.int32)
         .at[handover]
-        .set(held, unique_indices=True)
-        .reshape(owners, group_count, piece)
-    )
+        .set(jnp.arange(total_groups, dtype=jnp.int32))
+    )
+    forward = jnp.take(held, inverse, axis=0).reshape(owners, group_count, piece)
     arrived = lax.all_to_all(forward, "sub", 0, 0, tiled=True)
     landed = (
         arrived.reshape(2 * GROUP, splits, group_count, piece)

time: 281 us -> 284 us (1.011)
  waiting for transfers between devices: 93.4 us -> 77.7 us
  local copies, waits for them, and re-layouts: 61.1 us -> 75.6 us
  other arithmetic: 18.1 us -> 22.1 us
    gather x0 -> x1, local copies, waits for them, and re-layouts: none -> 20.2 us  [per_device(): jnp.take(held, inverse, axis=0).reshape(owners, group_count, piece)]
    all_to_all x1, waiting for transfers between devices: 69.9 us -> 54.2 us  [per_device(): lax.all_to_all(jnp.concatenate([spread, eval_spread], axis=1), 'sub', 0,...]
    all_to_all x0 -> x1, local copies, waits for them, and re-layouts: none -> 6.54 us  [per_device(): arrived = lax.all_to_all(forward, 'sub', 0, 0, tiled=True)]
    reshape x1 -> x0, local copies, waits for them, and re-layouts: 6.54 us -> none  [per_device(): arrived.reshape(2 * GROUP, splits, group_count, piece).transpose(2, 0, 1, 3)]
    scatter x1, local copies, waits for them, and re-layouts: 21.3 us -> 15.5 us  [per_device(): inverse = jnp.zeros((total_groups,), jnp.int32).at[handover].set(jnp.aran...]
    select_n x1 -> x2, other arithmetic: 0.01 us -> 3.95 us  [the longest x1 3.94 us: per_device(): jnp.take(held, inverse, axis=0).reshape(owners, group_count, piece)]
  transfers between devices with their start and end apart: 4 -> 4, of which waited for: 3 -> 3; matrix products, arithmetic and copies ran while one was open for 10% -> 15% of each run, Pallas kernels for 12% -> 12%
where the time goes in v1:
time: 284 us; the launch traced here: 281 us
  waiting for transfers between devices  77.7 us (27%)
  local copies, waits for them, and re-layouts  75.6 us (27%)
  Pallas kernels  64.6 us (23%)
  starting transfers between devices  33.7 us (12%)
  other arithmetic  22.1 us (8%)
  matrix products  6.67 us (2%)
    all_to_all x1, waiting for transfers between devices, per_device(): lax.all_to_all(jnp.concatenate([spread, eval_spread], axis=1), 'sub', 0,...  54.2 us
    pallas_call x1, Pallas kernels, second_round(): pl.pallas_call(lambda *refs: second_body(scale_in, scale_out, *refs), out...  32.5 us
    pallas_call x1, Pallas kernels, first_round(): pl.pallas_call(lambda *refs: first_body(scale_in, scale_out, *refs), out_...  32.1 us
    gather x1, local copies, waits for them, and re-layouts, per_device(): jnp.take(held, inverse, axis=0).reshape(owners, group_count, piece)  20.2 us
    all_to_all x1, waiting for transfers between devices, per_device(): arrived = lax.all_to_all(forward, 'sub', 0, 0, tiled=True)  19.1 us
    scatter x1, local copies, waits for them, and re-layouts, per_device(): inverse = jnp.zeros((total_groups,), jnp.int32).at[handover].set(jnp.aran...  15.5 us
    all_to_all x1, starting transfers between devices, per_device(): lax.all_to_all(summed, 'sub', 0, 0, tiled=True, axis_index_groups=same_pa...  11.9 us
    all_to_all x1, starting transfers between devices, per_device(): arrived = lax.all_to_all(forward, 'sub', 0, 0, tiled=True)  11.4 us
  transfers between devices with their start and end apart: 4, of which 3 were waited for; matrix products, arithmetic and copies ran while one was open for 15% of the time, Pallas kernels for 12%

profile of v1, /device:TPU:84, one launch (start us, length us, event | category | flops | bytes accessed | tf_op | source)
XLA Modules:
  0.0 281.1 jit_solution(11911795601510855740)
XLA Ops:
  2.2 32.1 %first_round.1 = (bf16[256,4096]{1,0:T(8,128)(2,1)}, bf16[256,4096]{1,0:T(8,128)(2,1)}) custom-call(s32[256,4]{1,0:T(8,128)} %get-tuple-element.17.refs_0_, bf16[512,4096]{1,0:T(8,128)(2,1)} %refs_2_.3, bf16[512,4096]{1,0:T(8,128)(2,1)} %refs_3_.3, f32[4096,256]{1,0:T(8,128)} %refs_3_.2, f32[4096,256]{1,0:T(8,128)} %refs_4_.1), custom_call_target="tpu_custom_call" | custom-call | flops 19327352832 | bytes 25165824 | tf_op jit(solution)/shard_map/first_round/pallas_call | solution.py:119
  34.3 2.9 %copy.17 = bf16[32,8,8,512]{3,0,2,1:T(8,128)(2,1)S(1)} copy(bf16[32,8,8,512]{3,1,2,0:T(8,128)(2,1)} %bitcast.38) | data formatting | bytes 4194304 | tf_op jit(solution)/shard_map/concatenate | solution.py:180
  37.2 2.5 copy.18
  42.0 3.1 %pad_maximum_fusion = bf16[128,48,512]{2,1,0:T(8,128)(2,1)} fusion(bf16[128,16,512]{2,1,0:T(8,128)(2,1)S(1)} %broadcast_in_dim.25, bf16[128,32,512]{2,1,0:T(8,128)(2,1)S(1)} %bitcast.35), kind=kLoop, calls=%fused_computation.2 | loop fusion | flops 12582912 | bytes 12582912 | tf_op jit(solution)/shard_map/concatenate | solution.py:194
  45.1 10.3 %all-to-all-start = ((bf16[128,48,512]{2,1,0:T(8,128)(2,1)}), bf16[128,48,512]{2,1,0:T(8,128)(2,1)}, u32[]{:S(2)}, u32[]{:S(2)}) async-start(bf16[128,48,512]{2,1,0:T(8,128)(2,1)} %pad_maximum_fusion), calls=%async_computation | async-start | bytes 12582912 | tf_op jit(solution)/shard_map/all_to_all | solution.py:193
  55.4 15.5 %scatter_custom_fusion = s32[4096]{0:T(1024)S(1)} fusion(s32[4096]{0:T(1024)S(1)} %compare_select_fusion.1, s32[4096]{0:T(1024)S(1)} %iota.7, s32[]{:T(128)} %constant.17.clone.1), kind=kCustom, calls=%fused_computation.26 | custom fusion | bytes 16388 | tf_op jit(solution)/shard_map/scatter | solution.py:202
  71.1 54.2 %all-to-all-done = bf16[128,48,512]{2,1,0:T(8,128)(2,1)} async-done(((bf16[128,48,512]{2,1,0:T(8,128)(2,1)}), bf16[128,48,512]{2,1,0:T(8,128)(2,1)}, u32[]{:S(2)}, u32[]{:S(2)}) %all-to-all-start) | async-done | bytes 6291488 | tf_op jit(solution)/shard_map/all_to_all | solution.py:193
  125.3 4.8 %slice.33 = bf16[128,32,512]{2,1,0:T(8,128)(2,1)} slice(bf16[128,48,512]{2,1,0:T(8,128)(2,1)} %all-to-all-done), slice={[0:128], [0:32], [0:512]} | slice | bytes 8388608 | tf_op jit(solution)/shard_map/slice | solution.py:196
  130.1 20.2 %gather_fusion = bf16[4096,512]{1,0:T(8,128)(2,1)} fusion(bf16[4096,512]{1,0:T(8,128)(2,1)} %bitcast.34, s32[4096]{0:T(1024)S(1)} %fusion.13), kind=kCustom, calls=%fused_computation | custom fusion | bytes 8404992 | tf_op jit(solution)/shard_map/jit(_take)/gather | solution.py:204
  150.3 3.9 %broadcast_select_fusion = bf16[128,32,512]{2,1,0:T(8,128)(2,1)} fusion(bf16[128,32,512]{2,1,0:T(8,128)(2,1)} %bitcast.36, pred[128,32]{1,0:T(8,128)(4,1)S(1)} %broadcast_in_dim.27), kind=kLoop, calls=%fused_computation.7 | loop fusion | flops 2097152 | bytes 8392704 | tf_op jit(solution)/shard_map/jit(_take)/select_n | solution.py:204
  154.3 11.4 %all-to-all-start.1 = ((bf16[128,32,512]{2,1,0:T(8,128)(2,1)}), bf16[128,32,512]{2,1,0:T(8,128)(2,1)}, u32[]{:S(2)}, u32[]{:S(2)}) async-start(bf16[128,32,512]{2,1,0:T(8,128)(2,1)} %broadcast_select_fusion), calls=%async_computation.1 | async-start | bytes 8388608 | tf_op jit(solution)/shard_map/all_to_all | solution.py:205
  165.7 3.2 %slice.30 = bf16[128,16,512]{2,1,0:T(8,128)(2,1)} slice(bf16[128,48,512]{2,1,0:T(8,128)(2,1)} %all-to-all-done), slice={[0:128], [32:48], [0:512]} | slice | bytes 4194304 | tf_op jit(solution)/shard_map/slice | solution.py:197
  168.9 4.2 %reshape.50 = bf16[256,4096]{1,0:T(8,128)(2,1)} reshape(bf16[128,16,512]{2,1,0:T(8,128)(2,1)} %slice.30) | data formatting | bytes 4194304 | tf_op jit(solution)/shard_map/reshape | solution.py:197
  173.2 6.7 %convolution_multiply_fusion = f32[256,4096]{1,0:T(8,128)} fusion(bf16[256,4096]{1,0:T(8,128)(2,1)} %get-tuple-element.11, bf16[256,4096]{1,0:T(8,128)(2,1)} %reshape.50, bf16[256,4096]{1,0:T(8,128)(2,1)S(1)} %copy-done.1), kind=kOutput, calls=%fused_computation.3 | convolution fusion | flops 1075445760 | bytes 10485760 | tf_op jit(solution)/shard_map/dot_general | solution.py:214
  179.8 5.8 %reshape.51 = f32[64,2,2,4096]{3,2,1,0:T(2,128)} reshape(f32[256,4096]{1,0:T(8,128)} %convolution_multiply_fusion) | data formatting | bytes 8388608 | tf_op jit(solution)/shard_map/reshape | solution.py:217
  185.7 5.9 %fusion = f32[64,2,4096]{2,1,0:T(2,128)} fusion(pred[]{:T(512)S(6)} %eq.6, f32[64,2,2,4096]{3,2,1,0:T(2,128)} %reshape.51), kind=kLoop, calls=%fused_computation.8 | loop fusion | flops 524288 | bytes 6291457 | tf_op jit(solution)/shard_map/jit(_where)/select_n | solution.py:219
  193.0 19.1 %all-to-all-done.1 = bf16[128,32,512]{2,1,0:T(8,128)(2,1)} async-done(((bf16[128,32,512]{2,1,0:T(8,128)(2,1)}), bf16[128,32,512]{2,1,0:T(8,128)(2,1)}, u32[]{:S(2)}, u32[]{:S(2)}) %all-to-all-start.1) | async-done | bytes 4194336 | tf_op jit(solution)/shard_map/all_to_all | solution.py:205
  212.2 6.5 %copy.26 = bf16[128,32,512]{2,0,1:T(8,128)(2,1)} copy(bf16[128,32,512]{2,1,0:T(8,128)(2,1)} %all-to-all-done.1) | data formatting | bytes 8388608 | tf_op jit(solution)/shard_map/all_to_all | solution.py:205
  218.7 7.4 %reshape.54.refs_4_ = bf16[32,16,4096]{2,1,0:T(8,128)(2,1)} reshape(bf16[32,16,8,512]{3,2,1,0:T(8,128)(2,1)} %bitcast.37) | data formatting | bytes 8388608 | tf_op jit(solution)/shard_map/reshape | solution.py:209
  226.1 4.4 %collective-permute-done = f32[64,2,4096]{2,1,0:T(2,128)S(1)} collective-permute-done((f32[64,2,4096]{2,1,0:T(2,128)}, f32[64,2,4096]{2,1,0:T(2,128)S(1)}, u32[]{:S(2)}, u32[]{:S(2)}) %collective-permute-start) | collective-permute-done | bytes 2097184 | tf_op jit(solution)/shard_map/ppermute | solution.py:222
  230.5 2.8 %add.35 = f32[64,2,4096]{2,1,0:T(2,128)} add(f32[64,2,4096]{2,1,0:T(2,128)S(1)} %fusion.1, f32[64,2,4096]{2,1,0:T(2,128)S(1)} %collective-permute-done) | non-fusion elementwise | flops 524288 | bytes 6291456 | tf_op jit(solution)/shard_map/add | solution.py:222
  233.3 11.9 %all-to-all-start.2 = ((f32[64,2,4096]{2,1,0:T(2,128)}), f32[64,2,4096]{2,1,0:T(2,128)}, u32[]{:S(2)}, u32[]{:S(2)}) async-start(f32[64,2,4096]{2,1,0:T(2,128)} %add.35), calls=%async_computation.2 | async-start | bytes 4194304 | tf_op jit(solution)/shard_map/all_to_all | solution.py:224
  245.8 32.5 %second_round.1 = (f32[4096,256]{1,0:T(8,128)}, f32[4096,256]{1,0:T(8,128)}) custom-call(s32[32]{0:T(128)} %iota.6.refs_0_, s32[256,4]{1,0:T(8,128)} %get-tuple-element.18.refs_1_, bf16[512,4096]{1,0:T(8,128)(2,1)} %refs_2_.3, bf16[512,4096]{1,0:T(8,128)(2,1)} %refs_3_.3, bf16[32,16,4096]{2,1,0:T(8,128)(2,1)} %reshape.54.refs_4_), custom_call_target="tpu_custom_call" | custom-call | flops 19327352832 | bytes 25165824 | tf_op jit(solution)/shard_map/second_round/pallas_call | solution.py:144
  278.3 2.8 %reduce_sum.9 = f32[2,4096]{1,0:T(2,128)} reduce(f32[64,2,4096]{2,1,0:T(2,128)} %all-to-all-done.2, f32[]{:T(128)} %constant.50.clone.1), dimensions={0}, to_apply=%region_1.2 | reduce | flops 516096 | bytes 2129924 | tf_op jit(solution)/shard_map/reduce_sum | solution.py:225
  (24 shorter events, 5.9 us)
Async XLA Ops:
  34.3 2.9 %copy-start.2 = (bf16[256,4096]{1,0:T(8,128)(2,1)S(1)}, bf16[256,4096]{1,0:T(8,128)(2,1)}, u32[]{:S(2)}) copy-start(bf16[256,4096]{1,0:T(8,128)(2,1)} %get-tuple-element.11) | copy-start | bytes 6291460
  34.3 5.4 %copy-start.3 = (bf16[2,4096]{1,0:T(2,128)(2,1)S(1)}, bf16[2,4096]{1,0:T(2,128)(2,1)}, u32[]{:S(2)}) copy-start(bf16[2,4096]{1,0:T(2,128)(2,1)} %param.12) | copy-start | bytes 49156
  45.1 10.3 %copy-start.4 = (s32[4096]{0:T(1024)S(1)}, s32[4096]{0:T(1024)}, u32[]{:S(2)}) copy-start(s32[4096]{0:T(1024)} %param.13) | copy-start | bytes 49156
  45.1 80.3 %all-to-all-start = ((bf16[128,48,512]{2,1,0:T(8,128)(2,1)}), bf16[128,48,512]{2,1,0:T(8,128)(2,1)}, u32[]{:S(2)}, u32[]{:S(2)}) async-start(bf16[128,48,512]{2,1,0:T(8,128)(2,1)} %pad_maximum_fusion), calls=%async_computation | async-start | bytes 12582912 | tf_op jit(solution)/shard_map/all_to_all | solution.py:193
  154.3 57.9 %all-to-all-start.1 = ((bf16[128,32,512]{2,1,0:T(8,128)(2,1)}), bf16[128,32,512]{2,1,0:T(8,128)(2,1)}, u32[]{:S(2)}, u32[]{:S(2)}) async-start(bf16[128,32,512]{2,1,0:T(8,128)(2,1)} %broadcast_select_fusion), calls=%async_computation.1 | async-start | bytes 8388608 | tf_op jit(solution)/shard_map/all_to_all | solution.py:205
  165.7 7.5 %copy-start.1 = (bf16[256,4096]{1,0:T(8,128)(2,1)S(1)}, bf16[256,4096]{1,0:T(8,128)(2,1)}, u32[]{:S(2)}) copy-start(bf16[256,4096]{1,0:T(8,128)(2,1)} %get-tuple-element.10) | copy-start | bytes 6291460
  185.7 5.9 %copy-start = (f32[64,2,2,4096]{3,2,1,0:T(2,128)S(1)}, f32[64,2,2,4096]{3,2,1,0:T(2,128)}, u32[]{:S(2)}) copy-start(f32[64,2,2,4096]{3,2,1,0:T(2,128)} %reshape.51) | copy-start | bytes 12582916
  226.1 4.4 %collective-permute-start = (f32[64,2,4096]{2,1,0:T(2,128)}, f32[64,2,4096]{2,1,0:T(2,128)S(1)}, u32[]{:S(2)}, u32[]{:S(2)}) collective-permute-start(f32[64,2,4096]{2,1,0:T(2,128)} %fusion), channel_id=1, source_target_pairs={{0,1},{1,0},{2,3},{3,2},{4,5},{5,4},{6,7},{7,6},{8,9},{9,8},{10,11... | collective-permute-start | bytes 6291464 | tf_op jit(solution)/shard_map/ppermute | solution.py:222
  233.3 44.9 %all-to-all-start.2 = ((f32[64,2,4096]{2,1,0:T(2,128)}), f32[64,2,4096]{2,1,0:T(2,128)}, u32[]{:S(2)}, u32[]{:S(2)}) async-start(f32[64,2,4096]{2,1,0:T(2,128)} %add.35), calls=%async_computation.2 | async-start | bytes 4194304 | tf_op jit(solution)/shard_map/all_to_all | solution.py:224
